TPU v7x, 32 devices: a whole 2x2x4 slice. The times are simulated.
32 devices in a mesh: grid: 8 (over z, x), mem: 4 (over y, core).
Axes of the slice: x: 2, y: 2, z: 4, core: 2. Of those that a mesh axis runs over, the one named last changes fastest.
Arguments:
- members: bfloat16 [80, 4, 16, 512], P('mem', None, 'grid'), may hold values from -0.8984375 to 0.8984375
- innovation: float32 [4, 16, 512], P(None, 'grid'), may hold values from -6 to 6
- observed_count: int32 [16, 512], P('grid'), may hold values from 0 to 3
- obs_precision: float32 [4], replicated, may hold values from 0.5 to 4
Outputs:
- recentred: bfloat16 [80, 4, 16, 512], P('mem', None, 'grid')
- increment: float32 [4, 16, 512], P('mem', 'grid')
All inputs are finite; a program needn't handle non-finite values.
Results may differ from a plain program's by a relative error of at most 0.0004.
Values may be sent and summed in bfloat16 or wider, within the bound.
No kernel may reach another device: no remote copies, remote signals or barrier semaphores. Data moves between devices by JAX's collectives and lax.ppermute only.
A program may use at most 64 MiB of HBM per device.

v0:
```python
import jax
import jax.numpy as jnp
from jax import lax
from jax.sharding import PartitionSpec as P

PASSES = 2
ITERS = 2
diffusion = 0.25


def padded(value, sides, width):
    for axis, dim in sides:
        devices, length = (lax.axis_size(axis), value.shape[dim])
        up = [(i, (i + 1) % devices) for i in range(devices - 1)]
        down = [(j, i) for i, j in up]
        last = lax.slice_in_dim(value, length - width, length, axis=dim)
        leading = lax.slice_in_dim(value, 0, width, axis=dim)
        before = lax.ppermute(last, axis, up)
        after = lax.ppermute(leading, axis, down)
        value = jnp.concatenate([before, value, after], axis=dim)
    return value


def smooth(field):
    for sweep_index in range(PASSES):
        extended = padded(field, (("grid", 2),), 1)
        centre = extended[:, :, 1:-1]
        field = centre + diffusion * (extended[:, :, :-2] + extended[:, :, 2:] - 2.0 * centre)
    for sweep_index in range(PASSES):
        field = field + diffusion * (jnp.roll(field, 1, 3) + jnp.roll(field, -1, 3) - 2.0 * field)
    return field


def member_total(product):
    summed = jnp.sum(product, axis=0)
    return summed


def norm_of(residual):
    return lax.psum(jnp.sum(residual * residual), ("grid", "mem"))


def local(members, innovation, observed_count, obs_precision):
    mem_index = lax.axis_index("mem")
    level_share = members.shape[1] // lax.axis_size("mem")
    perturbed = lax.all_to_all(members, "mem", split_axis=1, concat_axis=0, tiled=True)
    precision = lax.dynamic_slice_in_dim(obs_precision, mem_index * level_share, level_share, 0)
    local_innovation = lax.dynamic_slice_in_dim(innovation, mem_index * level_share, level_share, 0)
    weight = observed_count.astype(jnp.float32)[None] * precision[:, None, None]
    gradient = smooth(perturbed * (weight * local_innovation)[None])
    carried = jnp.zeros_like(gradient)
    residual = gradient
    direction = residual
    norm_now = norm_of(residual)
    for iteration in range(ITERS):
        smoothed = smooth(direction)
        total = member_total(perturbed * smoothed)
        back = smooth(perturbed * (weight * total)[None])
        image, smoothed = (direction + back, smoothed)
        step_size = norm_now / lax.psum(jnp.sum(direction * image), ("grid", "mem"))
        carried = carried + step_size * smoothed
        residual = residual - step_size * image
        if iteration + 1 < ITERS:
            norm_next = norm_of(residual)
            direction = residual + norm_next / norm_now * direction
            norm_now = norm_next
    increment = member_total(perturbed * carried)
    whole = lax.all_gather(increment, "mem", axis=0, tiled=True)
    recentred = (members.astype(jnp.float32) + whole[None]).astype(jnp.bfloat16)
    return (recentred, increment)


def smooth_rows(field):
    for sweep_index in range(PASSES):
        edge = jnp.zeros_like(field[..., :1, :])
        north = jnp.concatenate([edge, field[..., :-1, :]], axis=-2)
        south = jnp.concatenate([field[..., 1:, :], edge], axis=-2)
        field = field + diffusion * (north + south - 2.0 * field)
    for sweep_index in range(PASSES):
        field = field + diffusion * (jnp.roll(field, 1, -1) + jnp.roll(field, -1, -1) - 2.0 * field)
    return field


def all_sum(values):
    devices = lax.axis_size("grid") * lax.axis_size("mem")
    row = jnp.zeros((128,), jnp.float32).at[: values.shape[0]].set(values)
    gathered = lax.all_to_all(
        jnp.broadcast_to(row, (devices, 128)), ("grid", "mem"), 0, 0, tiled=True
    )
    return jnp.sum(gathered, axis=0)


def local_by_level(members, innovation, observed_count, obs_precision):
    grid_size = lax.axis_size("grid")
    mem_size = lax.axis_size("mem")
    count, levels, rows, nlon = members.shape
    copies = grid_size // levels
    nlat = rows * grid_size
    grid_index = lax.axis_index("grid")
    mem_index = lax.axis_index("mem")
    level = grid_index // copies
    chunk_level = [j // copies for j in range(grid_size)]
    sent = jnp.stack([members[:, l] for l in chunk_level], axis=0)
    got = lax.all_to_all(sent, "grid", 0, 0, tiled=True)
    mine = jnp.transpose(got, (1, 0, 2, 3)).reshape(count, nlat, nlon)
    extra = jnp.stack(
        [jnp.stack([innovation[l], observed_count.astype(jnp.float32)]) for l in chunk_level],
        axis=0,
    )
    extra = lax.all_to_all(extra, "grid", 0, 0, tiled=True)
    extra = jnp.transpose(extra, (1, 0, 2, 3)).reshape(2, nlat, nlon)
    precision = lax.dynamic_index_in_dim(obs_precision, level, 0, keepdims=False)
    weight = extra[1] * precision
    widened = mine.astype(jnp.float32)
    span = nlat // copies
    own = lax.broadcasted_iota(jnp.int32, (nlat, nlon), 0) // span == grid_index % copies
    first = mem_index == 0

    def squares(field):
        return jnp.sum(jnp.where(own[None], field * field, 0.0))

    def weighted(total):
        return jnp.where(first, jnp.sum(jnp.where(own, weight * total * total, 0.0)), 0.0)

    def project(field):
        return lax.psum(jnp.sum(widened * field, axis=0), "mem")

    residual = smooth_rows(widened * (weight * extra[0])[None])
    total1 = project(smooth_rows(residual))
    image = residual + smooth_rows(widened * (weight * total1)[None])
    projected_image = project(smooth_rows(image))
    first_sums = all_sum(jnp.stack([squares(residual), weighted(total1)]))
    norm_now = first_sums[0]
    step1 = norm_now / (norm_now + first_sums[1])
    residual_next = residual - step1 * image
    norm_next = all_sum(jnp.stack([squares(residual_next)]))[0]
    beta = norm_next / norm_now
    direction = residual_next + beta * residual
    total2 = total1 - step1 * projected_image + beta * total1
    second_sums = all_sum(jnp.stack([squares(direction), weighted(total2)]))
    step2 = norm_next / (second_sums[0] + second_sums[1])
    increment = step1 * total1 + step2 * total2
    spread = lax.all_to_all(increment.reshape(grid_size, rows, nlon), "grid", 0, 0, tiled=True)
    whole = spread.reshape(levels, copies, rows, nlon)[:, 0]
    share = levels // mem_size
    mine_out = lax.dynamic_slice_in_dim(whole, mem_index * share, share, 0)
    recentred = (members.astype(jnp.float32) + whole[None]).astype(jnp.bfloat16)
    return (recentred, mine_out)


def solution(mesh):
    placed = (P("mem", None, "grid", None), P(None, "grid", None), P("grid", None), P())
    grid_size, mem_size = (mesh.shape["grid"], mesh.shape["mem"])
    body = local

    def chosen(members, innovation, observed_count, obs_precision):
        levels = members.shape[1]
        fits = (
            grid_size % levels == 0
            and grid_size // levels <= 2
            and (levels % mem_size == 0)
            and (ITERS == 2)
        )
        pick = local_by_level if fits else body
        return jax.shard_map(
            pick,
            mesh=mesh,
            in_specs=placed,
            out_specs=(P("mem", None, "grid", None), P("mem", "grid", None)),
            check_vma=False,
        )(members, innovation, observed_count, obs_precision)

    return chosen
```

profile of v0, /device:TPU:0, one launch (start us, length us, event | category | flops | bytes accessed | tf_op | source)
XLA Modules:
  0.0 122.1 jit_solution(157087438368064626)
XLA Ops:
  0.6 0.7 convert_bitcast_fusion.1
  1.4 0.7 fusion.63
  6.9 7.3 %all-to-all-start.1 = ((f32[8,2,2,512]{3,2,1,0:T(2,128)}), f32[8,2,2,512]{3,2,1,0:T(2,128)S(1)}, u32[]{:S(2)}, u32[]{:S(2)}) async-start(f32[8,2,2,512]{3,2,1,0:T(2,128)} %constant_dynamic-update-slice_fusion), calls=%async_computation.1 | async-start | bytes 131072 | tf_op jit(solution)/shard_map/all_to_all | solution.py:110
  14.2 0.6 bitcast_dynamic-update-slice_fusion.4
  15.5 0.6 bitcast_dynamic-update-slice_fusion.6
  19.3 1.8 %all-to-all-done.1 = f32[8,2,2,512]{3,2,1,0:T(2,128)S(1)} async-done(((f32[8,2,2,512]{3,2,1,0:T(2,128)}), f32[8,2,2,512]{3,2,1,0:T(2,128)S(1)}, u32[]{:S(2)}, u32[]{:S(2)}) %all-to-all-start.1) | async-done | bytes 65568 | tf_op jit(solution)/shard_map/all_to_all | solution.py:110
  21.1 4.2 %all-to-all-start = ((bf16[8,20,2,512]{3,2,1,0:T(2,128)(2,1)}), bf16[8,20,2,512]{3,2,1,0:T(2,128)(2,1)S(1)}, u32[]{:S(2)}, u32[]{:S(2)}) async-start(bf16[8,20,2,512]{3,2,1,0:T(2,128)(2,1)} %bitcast_dynamic-update-slice_fusion.1), calls=%async_computation | async-start | bytes 655360 | tf_op jit(solution)/shard_map/all_to_all | solution.py:104
  26.7 0.7 fusion.61
  27.4 7.6 %all-to-all-done = bf16[8,20,2,512]{3,2,1,0:T(2,128)(2,1)S(1)} async-done(((bf16[8,20,2,512]{3,2,1,0:T(2,128)(2,1)}), bf16[8,20,2,512]{3,2,1,0:T(2,128)(2,1)S(1)}, u32[]{:S(2)}, u32[]{:S(2)}) %all-to-all-start) | async-done | bytes 327712 | tf_op jit(solution)/shard_map/all_to_all | solution.py:104
  38.1 0.9 select_reduce_fusion.2
  41.3 10.3 %psum.14 = f32[16,512]{1,0:T(8,128)S(1)} all-reduce(f32[16,512]{1,0:T(8,128)S(1)} %fusion.13), channel_id=1, replica_groups=mesh['grid'=8,'mem'=4] {'mem'}, use_global_device_ids=true, to_apply=%region_2.3 | all-reduce | flops 8192 | bytes 65536 | tf_op jit(solution)/shard_map/psum | solution.py:126
  51.6 0.7 select_reduce_fusion.3
  53.1 0.8 fusion.46
  53.9 1.1 fusion.45
  55.5 0.7 select_maximum_fusion.1
  56.9 3.8 %all-to-all-start.2 = ((f32[32,1,128]{2,1,0:T(1,128)}), f32[32,1,128]{2,1,0:T(1,128)S(1)}, u32[]{:S(2)}, u32[]{:S(2)}) async-start(f32[32,1,128]{2,1,0:T(1,128)} %broadcast_in_dim.42), calls=%async_computation.2 | async-start | bytes 32768 | tf_op jit(solution)/shard_map/all_to_all | solution.py:87
  60.7 1.5 %fusion.16 = f32[20,16,512]{2,1,0:T(8,128)S(1)} fusion(f32[20,16,512]{2,1,0:T(8,128)S(1)} %multiply_add_fusion.2, f32[20,16,511]{2,1,0:T(8,128)} %get-tuple-element.63, f32[20,16,1]{2,1,0:T(8,128)} %get-tuple-element.65, f32[20,16,1]{2,1,0:T(8,128)} %get-tuple-element.64, f32[20,16,511]{2,1,0:T(8,128)S(1)} %get-tuple-element.62), kind=kLoop, calls=%fused_computation.21 | loop fusion | flops 1146880 | bytes 2621440 | tf_op jit(solution)/shard_map/add | solution.py:80
  62.2 1.1 fusion.44
  63.3 0.8 fusion.43
  64.1 3.8 %all-to-all-done.2 = f32[32,1,128]{2,1,0:T(1,128)S(1)} async-done(((f32[32,1,128]{2,1,0:T(1,128)}), f32[32,1,128]{2,1,0:T(1,128)S(1)}, u32[]{:S(2)}, u32[]{:S(2)}) %all-to-all-start.2) | async-done | bytes 16416 | tf_op jit(solution)/shard_map/all_to_all | solution.py:87
  70.2 2.1 %select_reduce_fusion.1 = (f32[]{:T(128)}, f32[20,16,512]{2,1,0:T(8,128)S(1)}) fusion(f32[20,16,512]{2,1,0:T(8,128)S(1)} %get-tuple-element.41, f32[]{:T(128)S(6)} %div.31, pred[16,512]{1,0:T(8,128)(4,1)S(1)} %select_compare_fusion, f32[20,16,512]{2,1,0:T(8,128)S(1)} %fusion.16, f32[20,16,1]{2,1,0:T(8,128)} %get-tuple-element.59, ...), kind=kLoop, calls=%fused_computation.41 | loop fusion | flops 2129919 | bytes 3285000 | tf_op jit(solution)/shard_map/reduce_sum | solution.py:120
  72.4 0.6 scatter.19
  73.6 2.5 %all-to-all-start.3 = ((f32[32,1,128]{2,1,0:T(1,128)}), f32[32,1,128]{2,1,0:T(1,128)S(1)}, u32[]{:S(2)}, u32[]{:S(2)}) async-start(f32[32,1,128]{2,1,0:T(1,128)} %broadcast_in_dim.43), calls=%async_computation.3 | async-start | bytes 32768 | tf_op jit(solution)/shard_map/all_to_all | solution.py:87
  76.3 7.0 %all-to-all-done.3 = f32[32,1,128]{2,1,0:T(1,128)S(1)} async-done(((f32[32,1,128]{2,1,0:T(1,128)}), f32[32,1,128]{2,1,0:T(1,128)S(1)}, u32[]{:S(2)}, u32[]{:S(2)}) %all-to-all-start.3) | async-done | bytes 16416 | tf_op jit(solution)/shard_map/all_to_all | solution.py:87
  83.9 0.9 select_reduce_fusion
  86.7 10.4 %psum.15 = f32[16,512]{1,0:T(8,128)S(1)} all-reduce(f32[16,512]{1,0:T(8,128)S(1)} %fusion.28), channel_id=1, replica_groups=mesh['grid'=8,'mem'=4] {'mem'}, use_global_device_ids=true, to_apply=%region_9.10 | all-reduce | flops 8192 | bytes 65536 | tf_op jit(solution)/shard_map/psum | solution.py:126
  97.1 0.7 fusion.30
  98.4 0.7 select_maximum_fusion
  99.2 8.9 %all_to_all.33 = f32[32,1,128]{2,1,0:T(1,128)S(1)} all-to-all(f32[32,1,128]{2,1,0:T(1,128)S(1)} %broadcast_in_dim.44), channel_id=1, replica_groups=mesh['grid'=8,'mem'=4] {'grid','mem'}, dimensions={0} | all-to-all | bytes 32768 | tf_op jit(solution)/shard_map/all_to_all | solution.py:87
  110.7 3.3 %all-to-all-start.5 = ((f32[8,2,512]{2,1,0:T(2,128)}), f32[8,2,512]{2,1,0:T(2,128)S(1)}, u32[]{:S(2)}, u32[]{:S(2)}) async-start(f32[8,2,512]{2,1,0:T(2,128)} %reshape.159), calls=%async_computation.5 | async-start | bytes 65536 | tf_op jit(solution)/shard_map/all_to_all | solution.py:143
  114.1 6.6 %all-to-all-done.5 = f32[8,2,512]{2,1,0:T(2,128)S(1)} async-done(((f32[8,2,512]{2,1,0:T(2,128)}), f32[8,2,512]{2,1,0:T(2,128)S(1)}, u32[]{:S(2)}, u32[]{:S(2)}) %all-to-all-start.5) | async-done | bytes 32800 | tf_op jit(solution)/shard_map/all_to_all | solution.py:143
  120.7 0.8 add_convert_fusion
  (74 shorter events, 21.7 us)
Async XLA Ops:
  0.6 13.6 %copy-start = (bf16[20,4,2,512]{3,2,1,0:T(2,128)(2,1)S(1)}, bf16[20,4,2,512]{3,2,1,0:T(2,128)(2,1)}, u32[]{:S(2)}) copy-start(bf16[20,4,2,512]{3,2,1,0:T(2,128)(2,1)} %param.10) | copy-start | bytes 491524
  6.9 14.2 %all-to-all-start.1 = ((f32[8,2,2,512]{3,2,1,0:T(2,128)}), f32[8,2,2,512]{3,2,1,0:T(2,128)S(1)}, u32[]{:S(2)}, u32[]{:S(2)}) async-start(f32[8,2,2,512]{3,2,1,0:T(2,128)} %constant_dynamic-update-slice_fusion), calls=%async_computation.1 | async-start | bytes 131072 | tf_op jit(solution)/shard_map/all_to_all | solution.py:110
  21.1 13.9 %all-to-all-start = ((bf16[8,20,2,512]{3,2,1,0:T(2,128)(2,1)}), bf16[8,20,2,512]{3,2,1,0:T(2,128)(2,1)S(1)}, u32[]{:S(2)}, u32[]{:S(2)}) async-start(bf16[8,20,2,512]{3,2,1,0:T(2,128)(2,1)} %bitcast_dynamic-update-slice_fusion.1), calls=%async_computation | async-start | bytes 655360 | tf_op jit(solution)/shard_map/all_to_all | solution.py:104
  25.4 0.7 copy-start.1
  56.9 11.0 %all-to-all-start.2 = ((f32[32,1,128]{2,1,0:T(1,128)}), f32[32,1,128]{2,1,0:T(1,128)S(1)}, u32[]{:S(2)}, u32[]{:S(2)}) async-start(f32[32,1,128]{2,1,0:T(1,128)} %broadcast_in_dim.42), calls=%async_computation.2 | async-start | bytes 32768 | tf_op jit(solution)/shard_map/all_to_all | solution.py:87
  73.6 9.7 %all-to-all-start.3 = ((f32[32,1,128]{2,1,0:T(1,128)}), f32[32,1,128]{2,1,0:T(1,128)S(1)}, u32[]{:S(2)}, u32[]{:S(2)}) async-start(f32[32,1,128]{2,1,0:T(1,128)} %broadcast_in_dim.43), calls=%async_computation.3 | async-start | bytes 32768 | tf_op jit(solution)/shard_map/all_to_all | solution.py:87
  110.7 10.0 %all-to-all-start.5 = ((f32[8,2,512]{2,1,0:T(2,128)}), f32[8,2,512]{2,1,0:T(2,128)S(1)}, u32[]{:S(2)}, u32[]{:S(2)}) async-start(f32[8,2,512]{2,1,0:T(2,128)} %reshape.159), calls=%async_computation.5 | async-start | bytes 65536 | tf_op jit(solution)/shard_map/all_to_all | solution.py:143
where the time goes:
time: 123 us; the launch traced here: 122 us
  blocking collectives  29.6 us (24%)
  waiting for transfers between devices  26.8 us (22%)
  starting transfers between devices  21.2 us (17%)
  other arithmetic  19.5 us (16%)
  local copies, waits for them, and re-layouts  19.1 us (16%)
  between operations  5.99 us (5%)
    psum x2, blocking collectives, project(): return lax.psum(jnp.sum(widened * field, axis=0), 'mem')  20.7 us
    all_to_all x2, waiting for transfers between devices, all_sum(): lax.all_to_all(jnp.broadcast_to(row, (devices, 128)), ('grid', 'mem'), 0,...  10.7 us
    all_to_all x1, blocking collectives, all_sum(): lax.all_to_all(jnp.broadcast_to(row, (devices, 128)), ('grid', 'mem'), 0,...  8.95 us
    all_to_all x1, waiting for transfers between devices, local_by_level(): got = lax.all_to_all(sent, 'grid', 0, 0, tiled=True)  7.6 us
    all_to_all x1, starting transfers between devices, local_by_level(): extra = lax.all_to_all(extra, 'grid', 0, 0, tiled=True)  7.28 us
    all_to_all x1, waiting for transfers between devices, local_by_level(): lax.all_to_all(increment.reshape(grid_size, rows, nlon), 'grid', 0, 0, ti...  6.62 us
    all_to_all x2, starting transfers between devices, all_sum(): lax.all_to_all(jnp.broadcast_to(row, (devices, 128)), ('grid', 'mem'), 0,...  6.33 us
    unnamed x11, local copies, waits for them, and re-layouts  5.14 us
  transfers between devices with their start and end apart: 5, of which 5 were waited for; matrix products, arithmetic and copies ran while one was open for 8% of the time, Pallas kernels for 0%

commit v1 on v0

--- a/solution.py
+++ b/solution.py
@@ -123,7 +123,7 @@
         return jnp.where(first, jnp.sum(jnp.where(own, weight * total * total, 0.0)), 0.0)
 
     def project(field):
-        return lax.psum(jnp.sum(widened * field, axis=0), "mem")
+        return jnp.sum(lax.all_gather(jnp.sum(widened * field, axis=0), "mem"), axis=0)
 
     residual = smooth_rows(widened * (weight * extra[0])[None])
     total1 = project(smooth_rows(residual))

time: 123 us -> 118 us (0.959)
  blocking collectives: 29.6 us -> 19.7 us
  other arithmetic: 19.5 us -> 21.5 us
  local copies, waits for them, and re-layouts: 19.1 us -> 20.4 us
    psum x2 -> x0, blocking collectives: 20.7 us -> none  [project(): return lax.psum(jnp.sum(widened * field, axis=0), 'mem')]
    all_gather x0 -> x2, blocking collectives: none -> 10.8 us  [project(): lax.all_gather(jnp.sum(widened * field, axis=0), 'mem')]
    reduce_sum x3, other arithmetic: 0.06 us -> 2 us  [all_sum(): return jnp.sum(gathered, axis=0)]
    unnamed x11 -> x17, local copies, waits for them, and re-layouts: 5.14 us -> 6.46 us
  transfers between devices with their start and end apart: 5 -> 5, of which waited for: 5 -> 5; matrix products, arithmetic and copies ran while one was open for 8% -> 9% of each run, Pallas kernels for 0% -> 0%
where the time goes in v1:
time: 118 us; the launch traced here: 117 us
  waiting for transfers between devices  26.5 us (22%)
  starting transfers between devices  21.9 us (19%)
  other arithmetic  21.5 us (18%)
  local copies, waits for them, and re-layouts  20.4 us (17%)
  blocking collectives  19.7 us (17%)
  between operations  6.91 us (6%)
    all_gather x2, blocking collectives, project(): lax.all_gather(jnp.sum(widened * field, axis=0), 'mem')  10.8 us
    all_to_all x2, waiting for transfers between devices, all_sum(): lax.all_to_all(jnp.broadcast_to(row, (devices, 128)), ('grid', 'mem'), 0,...  10.5 us
    all_to_all x1, blocking collectives, all_sum(): lax.all_to_all(jnp.broadcast_to(row, (devices, 128)), ('grid', 'mem'), 0,...  8.87 us
    all_to_all x1, waiting for transfers between devices, local_by_level(): got = lax.all_to_all(sent, 'grid', 0, 0, tiled=True)  7.6 us
    all_to_all x1, starting transfers between devices, local_by_level(): extra = lax.all_to_all(extra, 'grid', 0, 0, tiled=True)  7.28 us
    all_to_all x2, starting transfers between devices, all_sum(): lax.all_to_all(jnp.broadcast_to(row, (devices, 128)), ('grid', 'mem'), 0,...  7 us
    all_to_all x1, waiting for transfers between devices, local_by_level(): lax.all_to_all(increment.reshape(grid_size, rows, nlon), 'grid', 0, 0, ti...  6.62 us
    unnamed x17, local copies, waits for them, and re-layouts  6.46 us
  transfers between devices with their start and end apart: 5, of which 5 were waited for; matrix products, arithmetic and copies ran while one was open for 9% of the time, Pallas kernels for 0%

profile of v1, /device:TPU:0, one launch (start us, length us, event | category | flops | bytes accessed | tf_op | source)
XLA Modules:
  0.0 117.0 jit_solution(1675162444592671773)
XLA Ops:
  0.6 0.7 convert_bitcast_fusion.1
  1.4 0.7 fusion.68
  6.9 7.3 %all-to-all-start.1 = ((f32[8,2,2,512]{3,2,1,0:T(2,128)}), f32[8,2,2,512]{3,2,1,0:T(2,128)S(1)}, u32[]{:S(2)}, u32[]{:S(2)}) async-start(f32[8,2,2,512]{3,2,1,0:T(2,128)} %constant_dynamic-update-slice_fusion), calls=%async_computation.1 | async-start | bytes 131072 | tf_op jit(solution)/shard_map/all_to_all | solution.py:110
  15.5 0.7 bitcast_dynamic-update-slice_fusion.6
  19.4 1.7 %all-to-all-done.1 = f32[8,2,2,512]{3,2,1,0:T(2,128)S(1)} async-done(((f32[8,2,2,512]{3,2,1,0:T(2,128)}), f32[8,2,2,512]{3,2,1,0:T(2,128)S(1)}, u32[]{:S(2)}, u32[]{:S(2)}) %all-to-all-start.1) | async-done | bytes 65568 | tf_op jit(solution)/shard_map/all_to_all | solution.py:110
  21.1 4.3 %all-to-all-start = ((bf16[8,20,2,512]{3,2,1,0:T(2,128)(2,1)}), bf16[8,20,2,512]{3,2,1,0:T(2,128)(2,1)S(1)}, u32[]{:S(2)}, u32[]{:S(2)}) async-start(bf16[8,20,2,512]{3,2,1,0:T(2,128)(2,1)} %bitcast_dynamic-update-slice_fusion.1), calls=%async_computation | async-start | bytes 655360 | tf_op jit(solution)/shard_map/all_to_all | solution.py:104
  26.8 0.7 fusion.66
  27.5 7.6 %all-to-all-done = bf16[8,20,2,512]{3,2,1,0:T(2,128)(2,1)S(1)} async-done(((bf16[8,20,2,512]{3,2,1,0:T(2,128)(2,1)}), bf16[8,20,2,512]{3,2,1,0:T(2,128)(2,1)S(1)}, u32[]{:S(2)}, u32[]{:S(2)}) %all-to-all-start) | async-done | bytes 327712 | tf_op jit(solution)/shard_map/all_to_all | solution.py:104
  38.1 1.0 select_reduce_fusion.2
  41.4 5.4 %all-gather = f32[64,512]{1,0:T(8,128)S(1)} all-gather(f32[16,512]{1,0:T(8,128)S(1)} %fusion.13), channel_id=2, replica_groups=mesh['grid'=8,'mem'=4] {'mem'}, dimensions={0}, use_global_device_ids=true | all-gather | bytes 163840 | tf_op jit(solution)/shard_map/all_gather | solution.py:126
  47.8 0.8 fusion.51
  48.5 1.1 fusion.50
  49.6 0.7 fusion.32
  50.9 0.8 select_maximum_fusion.1
  52.3 3.8 %all-to-all-start.2 = ((f32[32,1,128]{2,1,0:T(1,128)}), f32[32,1,128]{2,1,0:T(1,128)}, u32[]{:S(2)}, u32[]{:S(2)}) async-start(f32[32,1,128]{2,1,0:T(1,128)} %broadcast_in_dim.42), calls=%async_computation.2 | async-start | bytes 32768 | tf_op jit(solution)/shard_map/all_to_all | solution.py:87
  56.1 1.5 %fusion.16 = f32[20,16,512]{2,1,0:T(8,128)S(1)} fusion(f32[20,16,512]{2,1,0:T(8,128)S(1)} %multiply_add_fusion.2, f32[20,16,511]{2,1,0:T(8,128)} %get-tuple-element.61, f32[20,16,1]{2,1,0:T(8,128)} %get-tuple-element.63, f32[20,16,1]{2,1,0:T(8,128)} %get-tuple-element.62, f32[20,16,511]{2,1,0:T(8,128)S(1)} %get-tuple-element.60), kind=kLoop, calls=%fused_computation.21 | loop fusion | flops 1146880 | bytes 2621440 | tf_op jit(solution)/shard_map/add | solution.py:80
  57.6 1.1 fusion.49
  58.7 0.8 fusion.48
  59.5 3.6 %all-to-all-done.2 = f32[32,1,128]{2,1,0:T(1,128)} async-done(((f32[32,1,128]{2,1,0:T(1,128)}), f32[32,1,128]{2,1,0:T(1,128)}, u32[]{:S(2)}, u32[]{:S(2)}) %all-to-all-start.2) | async-done | bytes 16416 | tf_op jit(solution)/shard_map/all_to_all | solution.py:87
  63.1 0.7 reduce_sum.115
  66.4 2.1 %select_reduce_fusion.1 = (f32[]{:T(128)}, f32[20,16,512]{2,1,0:T(8,128)S(1)}) fusion(f32[20,16,512]{2,1,0:T(8,128)S(1)} %get-tuple-element.41, f32[]{:T(128)S(6)} %div.37, pred[16,512]{1,0:T(8,128)(4,1)S(1)} %select_compare_fusion.1, f32[20,16,512]{2,1,0:T(8,128)S(1)} %fusion.16, f32[20,16,1]{2,1,0:T(8,128)} %get-tuple-element.57, ...), kind=kLoop, calls=%fused_computation.41 | loop fusion | flops 2129919 | bytes 3285000 | tf_op jit(solution)/shard_map/reduce_sum | solution.py:120
  69.7 3.2 %all-to-all-start.3 = ((f32[32,1,128]{2,1,0:T(1,128)}), f32[32,1,128]{2,1,0:T(1,128)}, u32[]{:S(2)}, u32[]{:S(2)}) async-start(f32[32,1,128]{2,1,0:T(1,128)} %broadcast_in_dim.43), calls=%async_computation.3 | async-start | bytes 32768 | tf_op jit(solution)/shard_map/all_to_all | solution.py:87
  73.0 6.9 %all-to-all-done.3 = f32[32,1,128]{2,1,0:T(1,128)} async-done(((f32[32,1,128]{2,1,0:T(1,128)}), f32[32,1,128]{2,1,0:T(1,128)}, u32[]{:S(2)}, u32[]{:S(2)}) %all-to-all-start.3) | async-done | bytes 16416 | tf_op jit(solution)/shard_map/all_to_all | solution.py:87
  80.0 1.2 %reduce_sum.117 = f32[128]{0:T(128)} reduce(f32[32,1,128]{2,0,1:T(8,128)} %bitcast.20, f32[]{:T(128)} %constant.131.clone.1), dimensions={0,1}, to_apply=%region_6.7 | reduce | flops 3968 | bytes 16900 | tf_op jit(solution)/shard_map/reduce_sum | solution.py:90
  82.6 0.9 select_reduce_fusion
  85.4 5.4 %all-gather.1 = f32[64,512]{1,0:T(8,128)S(1)} all-gather(f32[16,512]{1,0:T(8,128)S(1)} %fusion.28), channel_id=3, replica_groups=mesh['grid'=8,'mem'=4] {'mem'}, dimensions={0}, use_global_device_ids=true | all-gather | bytes 163840 | tf_op jit(solution)/shard_map/all_gather | solution.py:126
  91.5 0.7 fusion.33
  93.5 8.9 %all_to_all.33 = f32[32,1,128]{2,1,0:T(1,128)S(1)} all-to-all(f32[32,1,128]{2,1,0:T(1,128)S(1)} %broadcast_in_dim.44), channel_id=1, replica_groups=mesh['grid'=8,'mem'=4] {'grid','mem'}, dimensions={0} | all-to-all | bytes 32768 | tf_op jit(solution)/shard_map/all_to_all | solution.py:87
  104.2 0.6 copy-done.3
  105.6 3.3 %all-to-all-start.5 = ((f32[8,2,512]{2,1,0:T(2,128)}), f32[8,2,512]{2,1,0:T(2,128)S(1)}, u32[]{:S(2)}, u32[]{:S(2)}) async-start(f32[8,2,512]{2,1,0:T(2,128)} %reshape.281), calls=%async_computation.5 | async-start | bytes 65536 | tf_op jit(solution)/shard_map/all_to_all | solution.py:143
  108.9 6.6 %all-to-all-done.5 = f32[8,2,512]{2,1,0:T(2,128)S(1)} async-done(((f32[8,2,512]{2,1,0:T(2,128)}), f32[8,2,512]{2,1,0:T(2,128)S(1)}, u32[]{:S(2)}, u32[]{:S(2)}) %all-to-all-start.5) | async-done | bytes 32800 | tf_op jit(solution)/shard_map/all_to_all | solution.py:143
  115.6 0.8 add_convert_fusion
  (88 shorter events, 24.2 us)
Async XLA Ops:
  0.6 13.6 %copy-start = (bf16[20,4,2,512]{3,2,1,0:T(2,128)(2,1)S(1)}, bf16[20,4,2,512]{3,2,1,0:T(2,128)(2,1)}, u32[]{:S(2)}) copy-start(bf16[20,4,2,512]{3,2,1,0:T(2,128)(2,1)} %param.10) | copy-start | bytes 491524
  6.9 14.2 %all-to-all-start.1 = ((f32[8,2,2,512]{3,2,1,0:T(2,128)}), f32[8,2,2,512]{3,2,1,0:T(2,128)S(1)}, u32[]{:S(2)}, u32[]{:S(2)}) async-start(f32[8,2,2,512]{3,2,1,0:T(2,128)} %constant_dynamic-update-slice_fusion), calls=%async_computation.1 | async-start | bytes 131072 | tf_op jit(solution)/shard_map/all_to_all | solution.py:110
  19.4 30.2 %copy-start.1 = (pred[8,2]{1,0:T(8,128)(4,1)}, pred[8,2]{1,0:T(8,128)(4,1)S(1)}, u32[]{:S(2)}) copy-start(pred[8,2]{1,0:T(8,128)(4,1)S(1)} %fusion.39) | copy-start | bytes 52
  21.1 14.0 %all-to-all-start = ((bf16[8,20,2,512]{3,2,1,0:T(2,128)(2,1)}), bf16[8,20,2,512]{3,2,1,0:T(2,128)(2,1)S(1)}, u32[]{:S(2)}, u32[]{:S(2)}) async-start(bf16[8,20,2,512]{3,2,1,0:T(2,128)(2,1)} %bitcast_dynamic-update-slice_fusion.1), calls=%async_computation | async-start | bytes 655360 | tf_op jit(solution)/shard_map/all_to_all | solution.py:104
  25.4 0.7 copy-start.4
  52.3 10.8 %all-to-all-start.2 = ((f32[32,1,128]{2,1,0:T(1,128)}), f32[32,1,128]{2,1,0:T(1,128)}, u32[]{:S(2)}, u32[]{:S(2)}) async-start(f32[32,1,128]{2,1,0:T(1,128)} %broadcast_in_dim.42), calls=%async_computation.2 | async-start | bytes 32768 | tf_op jit(solution)/shard_map/all_to_all | solution.py:87
  69.7 10.3 %all-to-all-start.3 = ((f32[32,1,128]{2,1,0:T(1,128)}), f32[32,1,128]{2,1,0:T(1,128)}, u32[]{:S(2)}, u32[]{:S(2)}) async-start(f32[32,1,128]{2,1,0:T(1,128)} %broadcast_in_dim.43), calls=%async_computation.3 | async-start | bytes 32768 | tf_op jit(solution)/shard_map/all_to_all | solution.py:87
  90.8 0.7 copy-start.2
  104.2 0.7 copy-start.3
  105.6 10.0 %all-to-all-start.5 = ((f32[8,2,512]{2,1,0:T(2,128)}), f32[8,2,512]{2,1,0:T(2,128)S(1)}, u32[]{:S(2)}, u32[]{:S(2)}) async-start(f32[8,2,512]{2,1,0:T(2,128)} %reshape.281), calls=%async_computation.5 | async-start | bytes 65536 | tf_op jit(solution)/shard_map/all_to_all | solution.py:143
